TPU v7x, 32 devices: a whole 2x2x4 slice. The times are simulated.
32 devices in a mesh: seq: 8 (over y, x, core), head: 4 (over z).
Axes of the slice: x: 2, y: 2, z: 4, core: 2. Of those that a mesh axis runs over, the one named last changes fastest.
Arguments:
- tokens: bfloat16 [8192, 1024], P(('seq', 'head')), may hold values from -6 to 6
- qkv_weight: bfloat16 [1024, 3, 1024], P(None, None, 'head'), may hold values from -0.1875 to 0.1875
- out_weight: bfloat16 [1024, 1024], P('head'), may hold values from -0.1875 to 0.1875
- up_weight: bfloat16 [1024, 2, 2816], P(None, None, 'head'), may hold values from -0.1875 to 0.1875
- down_weight: bfloat16 [2816, 1024], P('head'), may hold values from -0.109375 to 0.109375
- vocab_weight: bfloat16 [1024, 16384], P(None, 'head'), may hold values from -0.1875 to 0.1875
- persistent: bfloat16 [2, 16, 1024], P(None, None, 'head'), may hold values from -120 to 120
- norm_gains: float32 [3, 1024], replicated, may hold values from 0.5 to 1.5
- write_rate: float32 [8192, 8], P('seq', 'head'), may hold values from 0.02 to 0.2
- forget: float32 [128, 8], P('seq', 'head'), may hold values from 0 to 1
- momentum: float32 [128, 8], P('seq', 'head'), may hold values from 0.2 to 0.9
- prompt_spans: int32 [4], replicated, may hold values from 1 to 64, as said below
Outputs:
- logit_max: float32 [8192], P('seq')
- state_rms: float32 [4, 8], P(None, 'head')
Inputs may be any that keep to these rules, and one draw needn't show every extreme that they name: Prompt p holds prompt_spans[p] consecutive spans of 64 tokens, the prompts packed in order from token 0; they sum to 128, and prompt 1 is the longest, with exactly 64 spans.
All inputs are finite; a program needn't handle non-finite values.
Results may differ from a plain program's by a relative error of at most 0.0047.
Values may be sent and summed in bfloat16 or wider, within the bound.
No kernel may reach another device: no remote copies, remote signals or barrier semaphores. Data moves between devices by JAX's collectives and lax.ppermute only.
A program may use at most 128 MiB of HBM per device.

v0:
```python
import jax
import jax.numpy as jnp
from jax import lax
from jax.sharding import PartitionSpec as P

D = 1024
HS = 128
NPER = 16
SEG = 1024
CH = 64
SEQS = 4
eps_norm = 1e-05
eps_unit = 1e-06
score_scale = 10.0
masked_score = -1e30


def passed_along(array, axis, by):
    size = lax.axis_size(axis)
    pairs = [(i, i + by) for i in range(size) if 0 <= i + by < size]
    return lax.ppermute(array, axis, pairs)


def carried_in(part, axis, combine, identity):
    place = lax.axis_index(axis)
    gathered = jax.tree.map(lambda a: lax.all_gather(a, axis), part)
    state = jax.tree.map(lambda a, e: jnp.zeros_like(a) + jnp.asarray(e, a.dtype), part, identity)

    def one(step, state):
        return combine(
            state, jax.tree.map(lambda a: lax.dynamic_index_in_dim(a, step, 0, False), gathered)
        )

    return lax.fori_loop(0, place, one, state)


def rms_scale(values, gain):
    return values * lax.rsqrt(jnp.mean(values * values, axis=-1, keepdims=True) + eps_norm) * gain


def unit_rows(values):
    widened = values.astype(jnp.float32)
    return (
        widened * lax.rsqrt(jnp.sum(widened * widened, axis=-1, keepdims=True) + eps_unit)
    ).astype(jnp.bfloat16)


def segment_starts(positions, prompt_spans):
    prompt_ends = jnp.cumsum(prompt_spans)
    first_tokens = (prompt_ends - prompt_spans) * CH
    reached = positions[:, None] >= first_tokens[None, :]
    prompt_first = jnp.max(jnp.where(reached, first_tokens[None, :], 0), axis=1)
    return prompt_first + (positions - prompt_first) // SEG * SEG


def compose(later, earlier):
    return jnp.stack(
        [
            later[..., 0] * earlier[..., 0],
            later[..., 0] * earlier[..., 1] + later[..., 1] * earlier[..., 2],
            later[..., 2] * earlier[..., 2],
        ],
        axis=-1,
    )


def apply_map(coeffs, memory, moment):
    moved_memory = coeffs[:, 0, None, None] * memory + coeffs[:, 1, None, None] * moment
    return (moved_memory, coeffs[:, 2, None, None] * moment)


def chain_combine(earlier, later):
    moved_memory, moved_moment = apply_map(later[0], earlier[1], earlier[2])
    return (compose(later[0], earlier[0]), moved_memory + later[1], moved_moment + later[2])


def to_owners(local_rows, project):
    return project(lax.all_gather(local_rows, "head", axis=0, tiled=True), jnp.int32(0))


def from_owners(term, share_rows):
    return lax.psum_scatter(
        term(jnp.int32(0), share_rows * lax.axis_size("head")),
        "head",
        scatter_dimension=0,
        tiled=True,
    )


def local(
    tokens,
    qkv_weight,
    out_weight,
    up_weight,
    down_weight,
    vocab_weight,
    persistent,
    norm_gains,
    write_rate,
    forget,
    momentum,
    prompt_spans,
):
    share_rows = tokens.shape[0]
    head_count = lax.axis_size("head")
    seq_count = lax.axis_size("seq")
    block_rows = share_rows * head_count
    heads_here = write_rate.shape[1]
    current_width = heads_here * HS
    seq_index = lax.axis_index("seq")
    head_index = lax.axis_index("head")
    qkv_matrix = qkv_weight.reshape(D, 3 * current_width)
    highest = lax.Precision.HIGHEST

    def token_project(piece, start):
        normed = rms_scale(piece.astype(jnp.float32), norm_gains[0]).astype(jnp.bfloat16)
        projected = jnp.dot(normed, qkv_matrix, preferred_element_type=jnp.float32).astype(
            jnp.bfloat16
        )
        return projected

    gathered = to_owners(tokens, token_project)
    out_full = lax.all_gather(
        out_weight + (gathered[0, 0] * 0).astype(out_weight.dtype), "head", axis=0, tiled=True
    )
    down_full = lax.all_gather(
        down_weight + (gathered[0, 1] * 0).astype(down_weight.dtype), "head", axis=0, tiled=True
    )
    projected = gathered
    query_unit = unit_rows(projected[:, :current_width].reshape(block_rows, heads_here, HS))
    key_unit = unit_rows(
        projected[:, current_width : 2 * current_width].reshape(block_rows, heads_here, HS)
    )
    value_rows = projected[:, 2 * current_width :].reshape(block_rows, heads_here, HS)
    reach = SEG // block_rows
    moved_keys, moved_values = passed_along((key_unit, value_rows), "seq", 1)
    earlier_keys = [moved_keys]
    earlier_values = [moved_values]
    all_keys = jnp.concatenate(earlier_keys + [key_unit], axis=0)
    all_values = jnp.concatenate(earlier_values + [value_rows], axis=0)
    first_row = seq_index * block_rows
    query_positions = first_row + jnp.arange(block_rows, dtype=jnp.int32)
    key_positions = (
        first_row - reach * block_rows + jnp.arange((reach + 1) * block_rows, dtype=jnp.int32)
    )
    query_segments = segment_starts(query_positions, prompt_spans)
    key_segments = segment_starts(key_positions, prompt_spans)
    allowed = (
        (key_segments[None, :] == query_segments[:, None])
        & (key_positions[None, :] <= query_positions[:, None])
        & (key_positions[None, :] >= 0)
    )
    persist_keys = persistent[0].reshape(NPER, heads_here, HS)
    persist_values = persistent[1].reshape(NPER, heads_here, HS)
    scores = score_scale * jnp.einsum(
        "qhd,khd->hqk", query_unit, all_keys, preferred_element_type=jnp.float32
    )
    scores = jnp.where(allowed[None], scores, masked_score)
    extra = score_scale * jnp.einsum(
        "qhd,phd->hqp", query_unit, persist_keys, preferred_element_type=jnp.float32
    )
    top = jnp.maximum(jnp.max(scores, axis=-1), jnp.max(extra, axis=-1))[..., None]
    near = jnp.where(allowed[None], jnp.exp(scores - top), 0.0)
    far = jnp.exp(extra - top)
    total = jnp.sum(near, axis=-1, keepdims=True) + jnp.sum(far, axis=-1, keepdims=True)
    near_weights = (near / total).astype(jnp.bfloat16)
    far_weights = (far / total).astype(jnp.bfloat16)
    attended = jnp.einsum(
        "hqk,khd->qhd", near_weights, all_values, preferred_element_type=jnp.float32
    )
    attended = attended + jnp.einsum(
        "hqp,phd->qhd", far_weights, persist_values, preferred_element_type=jnp.float32
    )
    total_spans = block_rows // CH
    span_queries = query_unit.reshape(total_spans, CH, heads_here, HS)
    span_keys = key_unit.reshape(total_spans, CH, heads_here, HS)
    span_values = value_rows.reshape(total_spans, CH, heads_here, HS)
    span_rates = write_rate.reshape(total_spans, CH, heads_here)
    prompt_ends = jnp.cumsum(prompt_spans)
    first_spans = prompt_ends - prompt_spans
    span_ids = seq_index * total_spans + jnp.arange(total_spans, dtype=jnp.int32)
    keep = jnp.where(jnp.any(span_ids[:, None] == first_spans[None, :], axis=1), 0.0, 1.0).astype(
        jnp.float32
    )
    causal = (jnp.arange(CH)[:, None] >= jnp.arange(CH)[None, :]).astype(jnp.float32)
    values_wide = span_values.astype(jnp.float32)
    written = jnp.einsum(
        "cthi,cthj->chij",
        span_rates[..., None] * values_wide,
        span_keys.astype(jnp.float32),
        precision=highest,
    )
    affinity = jnp.einsum(
        "cthd,cshd->chts", span_queries, span_keys, preferred_element_type=jnp.float32
    )
    affinity = affinity * causal[None, None] * jnp.transpose(span_rates, (0, 2, 1))[:, :, None, :]
    local_recall = jnp.einsum("chts,cshi->cthi", affinity, values_wide, precision=highest)
    decay_memory = forget * keep[:, None]
    decay_moment = momentum * keep[:, None]
    identity_coeffs = jnp.tile(jnp.array([1.0, 0.0, 1.0], jnp.float32), (heads_here, 1))
    zero_state = jnp.zeros((heads_here, HS, HS), jnp.float32)

    def advance(carry, inputs):
        coeffs, memory, moment = carry
        current_written, memory_rate, moment_rate = inputs
        step_coeffs = jnp.stack([memory_rate, moment_rate, moment_rate], axis=-1)
        next_moment = moment_rate[:, None, None] * moment + current_written
        next_memory = (
            memory_rate[:, None, None] * memory
            + moment_rate[:, None, None] * moment
            + current_written
        )
        return ((compose(step_coeffs, coeffs), next_memory, next_moment), (coeffs, memory))

    (last_coeffs, last_memory, last_moment), (coeffs_before, memory_before) = lax.scan(
        advance, (identity_coeffs, zero_state, zero_state), (written, decay_memory, decay_moment)
    )
    _, incoming_memory, incoming_moment = carried_in(
        (last_coeffs, last_memory, last_moment),
        "seq",
        chain_combine,
        (identity_coeffs, zero_state, zero_state),
    )
    true_before = (
        memory_before
        + coeffs_before[..., 0, None, None] * incoming_memory[None]
        + coeffs_before[..., 1, None, None] * incoming_moment[None]
    )
    recalled = local_recall + jnp.einsum(
        "chij,cthj->cthi",
        true_before * keep[:, None, None, None],
        span_queries.astype(jnp.float32),
        precision=highest,
    )
    memory_after = jnp.concatenate([memory_before[1:], last_memory[None]], axis=0)
    coeffs_after = jnp.concatenate([coeffs_before[1:], last_coeffs[None]], axis=0)
    true_after = (
        memory_after
        + coeffs_after[..., 0, None, None] * incoming_memory[None]
        + coeffs_after[..., 1, None, None] * incoming_moment[None]
    )
    spread = jnp.sqrt(jnp.mean(true_after * true_after, axis=(2, 3)))
    hit_spans = span_ids[None, :] == (prompt_ends - 1)[:, None]
    state_slots = jnp.sum(jnp.where(hit_spans[:, :, None], spread[None], 0.0), axis=1)
    mixed = (
        (attended + recalled.reshape(block_rows, heads_here, HS))
        .astype(jnp.bfloat16)
        .reshape(block_rows, current_width)
    )
    ff_here = down_weight.shape[0]
    gate_up = up_weight.reshape(D, 2 * ff_here)

    def ffn_hidden(normed_rows):
        gated = jnp.dot(normed_rows, gate_up, preferred_element_type=jnp.float32)
        return (jax.nn.silu(gated[:, :ff_here]) * gated[:, ff_here:]).astype(jnp.bfloat16)

    def ffn_project(piece, start):
        return ffn_hidden(piece)

    pieces = mixed.reshape(head_count, share_rows, current_width)
    swapped = lax.all_to_all(pieces, "head", 0, 0, tiled=False)
    mixed_rows = jnp.transpose(swapped, (1, 0, 2)).reshape(share_rows, head_count * current_width)
    residual = tokens.astype(jnp.float32) + jnp.dot(
        mixed_rows, out_full, preferred_element_type=jnp.float32
    )
    residual = residual + (down_full[0, 0] * 0).astype(jnp.float32)
    hidden = to_owners(rms_scale(residual, norm_gains[1]).astype(jnp.bfloat16), ffn_project)
    hidden_pieces = hidden.reshape(head_count, share_rows, ff_here)
    hidden_swapped = lax.all_to_all(hidden_pieces, "head", 0, 0, tiled=False)
    hidden_rows = jnp.transpose(hidden_swapped, (1, 0, 2)).reshape(share_rows, head_count * ff_here)
    second = residual + jnp.dot(hidden_rows, down_full, preferred_element_type=jnp.float32)
    final = rms_scale(second, norm_gains[2]).astype(jnp.bfloat16)

    def vocab_maxima(piece, start):
        return jnp.max(jnp.dot(piece, vocab_weight, preferred_element_type=jnp.float32), axis=1)

    row_maxima = to_owners(final, vocab_maxima)
    logit_max = lax.pmax(row_maxima, "head")
    state_rms = jnp.sum(lax.all_gather(state_slots, "seq"), axis=0)
    return (logit_max, state_rms)


def solution(mesh):
    in_specs = (
        P(("seq", "head"), None),
        P(None, None, "head"),
        P("head", None),
        P(None, None, "head"),
        P("head", None),
        P(None, "head"),
        P(None, None, "head"),
        P(),
        P("seq", "head"),
        P("seq", "head"),
        P("seq", "head"),
        P(),
    )
    out_specs = (P("seq"), P(None, "head"))
    return jax.shard_map(local, mesh=mesh, in_specs=in_specs, out_specs=out_specs, check_vma=False)
```

profile of v0, /device:TPU:0, one launch (start us, length us, event | category | flops | bytes accessed | tf_op | source)
XLA Modules:
  0.0 514.6 jit_solution(8284672369578851746)
XLA Ops:
  8.1 2.7 copy.217
  13.5 44.8 %all-gather.14.cloned.1.call-done = bf16[1024,1024]{1,0:T(8,128)(2,1)} async-done(((bf16[256,1024]{1,0:T(8,128)(2,1)}), bf16[1024,1024]{1,0:T(8,128)(2,1)}) %all-gather.14.cloned.1.call-update) | async-done | bytes 2097168 | tf_op jit(solution)/shard_map/all_gather | solution.py:78
  60.6 3.3 fusion.23
  70.6 2.8 reshape.366
  73.4 3.5 copy.229
  77.0 3.1 convert_multiply_fusion.2
  80.1 3.5 fusion.43
  83.7 37.7 %while.34 = (s32[]{:T(128)}, f32[2,3]{0,1:T(4,128)S(1)}, f32[2,128,128]{2,1,0:T(8,128)S(1)}, f32[2,128,128]{2,1,0:T(8,128)S(1)}, f32[16,2,3]{2,1,0:T(2,128)}, /*...) while((s32[]{:T(128)}, f32[2,3]{0,1:T(4,128)S(1)}, ...), condition=%wide.region_12.13_spmd.clone, body=%wide.region_11.12_spmd.clone.sunk | while | flops 262167 | bytes 919916 | solution.py:215
  130.2 6.4 %and_and_fusion = pred[1024,2048]{1,0:T(8,128)(4,1)} fusion(s32[2048]{0:T(1024)S(1)} %iota_add_fusion, s32[2048]{0:T(1024)S(1)} %fusion.57, s32[1024]{0:T(1024)S(1)} %iota_add_fusion.1, s32[1024]{0:T(1024)S(1)} %fusion.64, pred[2048]{0:T(1024)(128)(4,1)S(1)} %fusion.61), kind=kLoop, calls=%fused_computation.25 | loop fusion | flops 8388608 | bytes 2123776 | tf_op jit(solution)/shard_map/and | solution.py:149
  136.7 9.0 %all-gather.4 = f32[8,2,3]{2,1,0:T(2,128)} all-gather(f32[1,2,3]{2,1,0:T(2,128)S(1)} %bitcast.132), channel_id=2, replica_groups=mesh['seq'=8,'head'=4] {'seq'}, dimensions={0}, use_global_device_ids=true | all-gather | bytes 216 | tf_op jit(solution)/shard_map/all_gather | solution.py:26
  149.8 3.5 collective-permute-start.1
  153.3 2.9 reshape.365
  160.3 3.5 copy.226
  164.6 4.1 collective-permute-start
  173.2 3.3 fusion.30
  176.5 4.9 fusion.3
  181.5 5.6 %fusion.4 = f32[2,1024]{1,0:T(2,128)S(1)} fusion(f32[2,1024,2048]{2,1,0:T(8,128)S(1)} %get-tuple-element.215, f32[2,1024]{1,0:T(2,128)S(1)} %max.9, pred[1024,2048]{1,0:T(8,128)(4,1)S(1)} %copy-done.5), kind=kLoop, calls=%fused_computation.24 | loop fusion | flops 20969472 | bytes 18890752 | tf_op jit(solution)/shard_map/reduce_sum | solution.py:165
  189.7 4.3 fusion.27
  198.4 11.1 %fusion.35 = bf16[1024,2,128]{0,2,1:T(8,128)(2,1)} fusion(f32[1024,2,128]{0,2,1:T(8,128)} %copy.242, f32[1024,2,128]{0,2,1:T(8,128)} %convolution_bitcast_fusion, f32[2,1024,2048]{2,1,0:T(8,128)} %copy-done.3, f32[2,1024]{1,0:T(2,128)S(1)} %add.232, f32[2,1024]{1,0:T(2,128)S(1)} %max.9, pred[1024,2048]{1,0:T(8,128)(4,1)} %and_and_fusion, ...), kind=kOutput, calls=%fused_computation.61 | convolution fusion | flops 1101791232 | bytes 22560768 | tf_op jit(solution)/shard_map/hqk,khd->qhd/dot_general | solution.py:168
  213.7 4.1 all-to-all-start
  217.9 72.7 %all-gather.18.cloned.1.call-done = bf16[2816,1024]{1,0:T(8,128)(2,1)} async-done(((bf16[704,1024]{1,0:T(8,128)(2,1)}), bf16[2816,1024]{1,0:T(8,128)(2,1)}) %all-gather.18.cloned.1.call-update) | async-done | bytes 5767184 | tf_op jit(solution)/shard_map/all_gather | solution.py:126
  292.5 43.8 %all-gather.16.cloned.1.call-done = bf16[1024,1024]{1,0:T(8,128)(2,1)} async-done(((bf16[256,1024]{1,0:T(8,128)(2,1)}), bf16[1024,1024]{1,0:T(8,128)(2,1)}) %all-gather.16.cloned.1.call-update) | async-done | bytes 2097168 | tf_op jit(solution)/shard_map/all_gather | solution.py:123
  336.3 2.7 multiply_reduce_fusion.1
  341.0 44.8 %all-gather.20.cloned.1.call-done = bf16[1024,1024]{1,0:T(8,128)(2,1)} async-done(((bf16[256,1024]{1,0:T(8,128)(2,1)}), bf16[1024,1024]{1,0:T(8,128)(2,1)}) %all-gather.20.cloned.1.call-update) | async-done | bytes 2097168 | tf_op jit(solution)/shard_map/all_gather | solution.py:78
  385.8 5.0 fusion.77
  395.7 38.3 %all_to_all.10 = bf16[4,256,704]{1,2,0:T(8,128)(2,1)S(1)} all-to-all(bf16[4,256,704]{1,2,0:T(8,128)(2,1)} %copy.245), channel_id=1, replica_groups=mesh['seq'=8,'head'=4] {'head'}, dimensions={0} | all-to-all | bytes 2883584 | tf_op jit(solution)/shard_map/all_to_all | solution.py:269
  434.0 4.4 multiply_reduce_fusion
  439.8 3.0 slice.102
  445.4 8.9 %all-gather.5 = f32[8,4,2]{1,2,0:T(2,128)S(1)} all-gather(f32[1,4,2]{1,2,0:T(2,128)S(1)} %bitcast.136), channel_id=5, replica_groups=mesh['seq'=8,'head'=4] {'seq'}, dimensions={0}, use_global_device_ids=true | all-gather | bytes 288 | tf_op jit(solution)/shard_map/all_gather | solution.py:279
  454.9 29.7 %all-gather.22.cloned.1.call-done = bf16[1024,1024]{1,0:T(8,128)(2,1)} async-done(((bf16[256,1024]{1,0:T(8,128)(2,1)}), bf16[1024,1024]{1,0:T(8,128)(2,1)}) %all-gather.22.cloned.1.call-update) | async-done | bytes 2097168 | tf_op jit(solution)/shard_map/all_gather | solution.py:78
  484.6 12.9 %convolution_reduce_fusion = f32[1024]{0:T(1024)S(1)} fusion(bf16[1024,1024]{1,0:T(8,128)(2,1)} %all-gather.22.cloned.1.call-done, bf16[1024,4096]{1,0:T(8,128)(2,1)} %param.22), kind=kOutput, calls=%fused_computation.32 | convolution fusion | flops 8594127872 | bytes 10489856 | tf_op jit(solution)/shard_map/dot_general | solution.py:275
  497.5 10.1 %pmax.7 = f32[1024]{0:T(1024)} all-reduce(f32[1024]{0:T(1024)S(1)} %convolution_reduce_fusion), channel_id=1, replica_groups=mesh['seq'=8,'head'=4] {'head'}, use_global_device_ids=true, to_apply=%region_18.19 | all-reduce | flops 1024 | bytes 8192 | tf_op jit(solution)/shard_map/pmax | solution.py:278
  (297 shorter events, 94.9 us)
Async XLA Ops:
  7.2 378.6 %copy-start = (bf16[1024,2,704]{0,2,1:T(8,128)(2,1)S(1)}, bf16[1024,2,704]{0,2,1:T(8,128)(2,1)}, u32[]{:S(2)}) copy-start(bf16[1024,2,704]{0,2,1:T(8,128)(2,1)} %param.20) | copy-start | bytes 8650756
  7.2 4.7 copy-start.36
  7.2 4.8 copy-start.34
  7.2 4.9 copy-start.35
  7.2 5.6 %copy-start.28 = (f32[3,1024]{1,0:T(4,128)S(1)}, f32[3,1024]{1,0:T(4,128)}, u32[]{:S(2)}) copy-start(f32[3,1024]{1,0:T(4,128)} %param.24) | copy-start | bytes 36868
  7.2 51.1 %all-gather.14.cloned.1.call-start = ((), (), s32[]{:S(2)}) async-start(), calls=%async_computation.2 | async-start | bytes 2621440 | tf_op jit(solution)/shard_map/all_gather | solution.py:78
  8.0 181.0 %all-gather.24.cloned.1.call-start = ((), (), s32[]{:S(2)}) async-start(), calls=%async_computation.7 | async-start | bytes 1179648 | tf_op jit(solution)/shard_map/all_gather | solution.py:26
  76.9 6.7 %copy-start.17 = (f32[1024,2]{0,1:T(2,128)}, f32[1024,2]{0,1:T(2,128)S(1)}, u32[]{:S(2)}) copy-start(f32[1024,2]{0,1:T(2,128)S(1)} %add_rsqrt_fusion) | copy-start | bytes 24580
  122.0 66.9 %all-gather.26.cloned.1.call-start = ((), (), s32[]{:S(2)}) async-start(), calls=%async_computation.8 | async-start | bytes 1179648 | tf_op jit(solution)/shard_map/all_gather | solution.py:26
  122.7 167.9 %all-gather.18.cloned.1.call-start = ((), (), s32[]{:S(2)}) async-start(), calls=%async_computation.4 | async-start | bytes 7208960 | tf_op jit(solution)/shard_map/all_gather | solution.py:126
  127.5 208.8 %all-gather.16.cloned.1.call-start = ((), (), s32[]{:S(2)}) async-start(), calls=%async_computation.3 | async-start | bytes 2621440 | tf_op jit(solution)/shard_map/all_gather | solution.py:123
  130.2 18.0 %copy-start.18 = (f32[1024,2]{0,1:T(2,128)S(1)}, f32[1024,2]{0,1:T(2,128)}, u32[]{:S(2)}) copy-start(f32[1024,2]{0,1:T(2,128)} %copy-done.17) | copy-start | bytes 24580
  136.7 16.5 %copy-start.29 = (f32[2,3]{1,0:T(2,128)}, f32[2,3]{1,0:T(2,128)S(1)}, u32[]{:S(2)}) copy-start(f32[2,3]{1,0:T(2,128)S(1)} %copy.238) | copy-start | bytes 76
  149.8 26.7 %collective-permute-start.1 = (bf16[1024,2,128]{2,0,1:T(8,128)(2,1)S(1)}, bf16[1024,2,128]{2,0,1:T(8,128)(2,1)}, u32[]{:S(2)}, u32[]{:S(2)}) collective-permute-start(bf16[1024,2,128]{2,0,1:T(8,128)(2,1)S(1)} %multiply_convert_fusion.4), channel_id=1, source_target_pairs={{0,4},{4,8},{8,12},{12,16},{16,20},{20,24},{24,28},{1,5},{5,9},{9,... | collective-permute-start | bytes 1572872 | tf_op jit(solution)/shard_map/ppermute | solution.py:21
  153.2 5.5 %copy-start.15 = (f32[16,2,3]{2,1,0:T(2,128)S(1)}, f32[16,2,3]{2,1,0:T(2,128)}, u32[]{:S(2)}) copy-start(f32[16,2,3]{2,1,0:T(2,128)} %get-tuple-element.113) | copy-start | bytes 1156
  158.7 5.1 copy-start.21
  163.8 7.4 %copy-start.19 = (f32[1024,2]{0,1:T(2,128)}, f32[1024,2]{0,1:T(2,128)S(1)}, u32[]{:S(2)}) copy-start(f32[1024,2]{0,1:T(2,128)S(1)} %add_rsqrt_fusion.1) | copy-start | bytes 24580
  164.6 33.8 %collective-permute-start = (bf16[1024,2,128]{0,2,1:T(8,128)(2,1)}, bf16[1024,2,128]{0,2,1:T(8,128)(2,1)}, u32[]{:S(2)}, u32[]{:S(2)}) collective-permute-start(bf16[1024,2,128]{0,2,1:T(8,128)(2,1)} %bitcast.5), channel_id=1, source_target_pairs={{0,4},{4,8},{8,12},{12,16},{16,20},{20,24},{24,28},{1,5},{5,9},{9,... | collective-permute-start | bytes 1572872 | tf_op jit(solution)/shard_map/ppermute | solution.py:21
  171.3 5.2 %copy-start.5 = (pred[1024,2048]{1,0:T(8,128)(4,1)S(1)}, pred[1024,2048]{1,0:T(8,128)(4,1)}, u32[]{:S(2)}) copy-start(pred[1024,2048]{1,0:T(8,128)(4,1)} %and_and_fusion) | copy-start | bytes 6291460
  171.3 5.2 %copy-start.12 = (f32[1024,2,128]{2,0,1:T(8,128)S(1)}, f32[1024,2,128]{2,0,1:T(8,128)}, u32[]{:S(2)}) copy-start(f32[1024,2,128]{2,0,1:T(8,128)} %copy.218) | copy-start | bytes 3145732
  171.3 5.2 %copy-start.20 = (f32[1024,2]{0,1:T(2,128)S(1)}, f32[1024,2]{0,1:T(2,128)}, u32[]{:S(2)}) copy-start(f32[1024,2]{0,1:T(2,128)} %copy-done.19) | copy-start | bytes 24580
  181.4 6.1 %copy-start.3 = (f32[2,1024,2048]{2,1,0:T(8,128)}, f32[2,1024,2048]{2,1,0:T(8,128)S(1)}, u32[]{:S(2)}) copy-start(f32[2,1024,2048]{2,1,0:T(8,128)S(1)} %get-tuple-element.215) | copy-start | bytes 50331652
  181.5 6.1 %copy-start.24 = (bf16[16,2,128]{2,1,0:T(2,128)(2,1)S(1)}, bf16[16,2,128]{2,1,0:T(2,128)(2,1)}, u32[]{:S(2)}) copy-start(bf16[16,2,128]{2,1,0:T(2,128)(2,1)} %reshape_squeeze.7) | copy-start | bytes 24580
  189.7 4.3 copy-start.7
  189.7 4.4 copy-start.9
  213.7 78.8 %all-to-all-start = ((bf16[4,256,256]{1,2,0:T(8,128)(2,1)}), bf16[4,256,256]{1,2,0:T(8,128)(2,1)}, u32[]{:S(2)}, u32[]{:S(2)}) async-start(bf16[4,256,256]{1,2,0:T(8,128)(2,1)} %copy.243), calls=%async_computation | async-start | bytes 1048576 | tf_op jit(solution)/shard_map/all_to_all | solution.py:261
  217.9 167.9 %all-gather.20.cloned.1.call-start = ((), (), s32[]{:S(2)}) async-start(), calls=%async_computation.5 | async-start | bytes 2621440 | tf_op jit(solution)/shard_map/all_gather | solution.py:78
  336.3 3.7 copy-start.26
  340.9 143.6 %all-gather.22.cloned.1.call-start = ((), (), s32[]{:S(2)}) async-start(), calls=%async_computation.6 | async-start | bytes 2621440 | tf_op jit(solution)/shard_map/all_gather | solution.py:78
  395.7 38.3 %copy-start.11 = (f32[256,1024]{1,0:T(8,128)S(1)}, f32[256,1024]{1,0:T(8,128)}, u32[]{:S(2)}) copy-start(f32[256,1024]{1,0:T(8,128)} %copy-done.10) | copy-start | bytes 3145732
  434.0 4.5 copy-start.25
  439.5 3.6 copy-start.2
  (19 other events, 29.3 us)
Sparse Core Ops, SparseCore 0:
  9.6 48.6 all-gather.13
  122.1 22.2 all-gather.23
  146.3 24.1 all-gather.25
  171.9 118.6 all-gather.17
  292.1 44.1 all-gather.15
  341.1 44.6 all-gather.19
  439.6 44.9 all-gather.21
where the time goes:
time: 524 us; the launch traced here: 515 us
  waiting for transfers between devices  237 us (45%)
  blocking collectives  66.2 us (13%)
  other arithmetic  62 us (12%)
  local copies, waits for them, and re-layouts  60.5 us (12%)
  matrix products  59.5 us (11%)
  between operations  16.9 us (3%)
  starting transfers between devices  12 us (2%)
    all_gather x3, waiting for transfers between devices, to_owners(): lax.all_gather(local_rows, 'head', axis=0, tiled=True)  119 us
    all_gather x1, waiting for transfers between devices, local(): lax.all_gather(down_weight + (gathered[0, 1] * 0).astype(down_weight.dtyp...  72.7 us
    all_gather x1, waiting for transfers between devices, local(): lax.all_gather(out_weight + (gathered[0, 0] * 0).astype(out_weight.dtype)...  43.8 us
    all_to_all x1, blocking collectives, local(): hidden_swapped = lax.all_to_all(hidden_pieces, 'head', 0, 0, tiled=False)  38.3 us
    convert_element_type x6, local copies, waits for them, and re-layouts, unit_rows(): widened = values.astype(jnp.float32)  17.8 us
    add x16, other arithmetic, advance(): next_moment = moment_rate[:, None, None] * moment + current_written  16 us
    dot_general x1, matrix products, vocab_maxima(): jnp.dot(piece, vocab_weight, preferred_element_type=jnp.float32)  12.9 us
    dot_general x1, matrix products, local(): jnp.einsum('hqk,khd->qhd', near_weights, all_values, preferred_element_ty...  11.1 us
  transfers between devices with their start and end apart: 10, of which 5 were waited for; matrix products, arithmetic and copies ran while one was open for 16% of the time, Pallas kernels for 0%

commit v1 on v0

--- a/solution.py
+++ b/solution.py
@@ -123,8 +123,17 @@
     out_full = lax.all_gather(
         out_weight + (gathered[0, 0] * 0).astype(out_weight.dtype), "head", axis=0, tiled=True
     )
-    down_full = lax.all_gather(
-        down_weight + (gathered[0, 1] * 0).astype(down_weight.dtype), "head", axis=0, tiled=True
+    down_full = jnp.concatenate(
+        lax.all_to_all(
+            jnp.stack(
+                [down_weight + (gathered[0, 1] * 0).astype(down_weight.dtype)]
+                * lax.axis_size("head")
+            ),
+            "head",
+            0,
+            0,
+        ),
+        axis=0,
     )
     projected = gathered
     query_unit = unit_rows(projected[:, :current_width].reshape(block_rows, heads_here, HS))

time: 524 us -> 530 us (1.011)
  waiting for transfers between devices: 237 us -> 248 us
  local copies, waits for them, and re-layouts: 60.5 us -> 52.2 us
    all_to_all x0 -> x1, waiting for transfers between devices: none -> 116 us  [local(): lax.all_to_all(jnp.stack([down_weight + (gathered[0, 1] * 0).astype(down_...]
    all_gather x1 -> x0, waiting for transfers between devices: 72.7 us -> none  [local(): lax.all_gather(down_weight + (gathered[0, 1] * 0).astype(down_weight.dtyp...]
    all_gather x1, waiting for transfers between devices: 43.8 us -> 0.01 us  [local(): lax.all_gather(out_weight + (gathered[0, 0] * 0).astype(out_weight.dtype)...]
    all_to_all x1, waiting for transfers between devices: 0.01 us -> 12.1 us  [local(): swapped = lax.all_to_all(pieces, 'head', 0, 0, tiled=False)]
    dynamic_update_slice x16, local copies, waits for them, and re-layouts: 8.94 us -> 0.16 us  [local(): lax.scan(advance, (identity_coeffs, zero_state, zero_state), (written, de...]
where the time goes in v1:
time: 530 us; the launch traced here: 520 us
  waiting for transfers between devices  248 us (47%)
  blocking collectives  67 us (13%)
  other arithmetic  59.7 us (11%)
  matrix products  59.4 us (11%)
  local copies, waits for them, and re-layouts  52.2 us (10%)
  between operations  16.9 us (3%)
  starting transfers between devices  16.2 us (3%)
    all_gather x3, waiting for transfers between devices, to_owners(): lax.all_gather(local_rows, 'head', axis=0, tiled=True)  119 us
    all_to_all x1, waiting for transfers between devices, local(): lax.all_to_all(jnp.stack([down_weight + (gathered[0, 1] * 0).astype(down_...  116 us
    all_to_all x1, blocking collectives, local(): hidden_swapped = lax.all_to_all(hidden_pieces, 'head', 0, 0, tiled=False)  38.3 us
    convert_element_type x6, local copies, waits for them, and re-layouts, unit_rows(): widened = values.astype(jnp.float32)  17.8 us
    add x16, other arithmetic, advance(): next_moment = moment_rate[:, None, None] * moment + current_written  16 us
    dot_general x1, matrix products, vocab_maxima(): jnp.dot(piece, vocab_weight, preferred_element_type=jnp.float32)  12.9 us
    all_to_all x1, waiting for transfers between devices, local(): swapped = lax.all_to_all(pieces, 'head', 0, 0, tiled=False)  12.1 us
    dot_general x1, matrix products, local(): jnp.einsum('hqk,khd->qhd', near_weights, all_values, preferred_element_ty...  11.2 us
  transfers between devices with their start and end apart: 10, of which 5 were waited for; matrix products, arithmetic and copies ran while one was open for 16% of the time, Pallas kernels for 0%

profile of v1, /device:TPU:0, one launch (start us, length us, event | category | flops | bytes accessed | tf_op | source)
XLA Modules:
  0.0 520.3 jit_solution(1867166601838208267)
XLA Ops:
  13.5 44.8 %all-gather.13.cloned.1.call-done = bf16[1024,1024]{1,0:T(8,128)(2,1)} async-done(((bf16[256,1024]{1,0:T(8,128)(2,1)}), bf16[1024,1024]{1,0:T(8,128)(2,1)}) %all-gather.13.cloned.1.call-update) | async-done | bytes 2097168 | tf_op jit(solution)/shard_map/all_gather | solution.py:78
  60.6 3.3 fusion.23
  70.0 2.8 reshape.370
  72.9 3.5 copy.230
  76.5 3.1 convert_multiply_fusion.2
  79.5 3.5 fusion.51
  83.1 29.2 %while.34 = (s32[]{:T(128)}, f32[2,3]{0,1:T(4,128)S(1)}, f32[2,128,128]{2,1,0:T(8,128)S(1)}, f32[2,128,128]{2,1,0:T(8,128)S(1)}, f32[16,2,3]{2,1,0:T(2,128)S(1)}...) while((s32[]{:T(128)}, f32[2,3]{0,1:T(4,128)S(1)}, ...), condition=%wide.region_12.13_spmd.clone, body=%wide.region_11.12_spmd.clone.sunk | while | flops 262167 | bytes 920408 | solution.py:224
  114.6 6.5 %and_and_fusion = pred[1024,2048]{1,0:T(8,128)(4,1)} fusion(s32[2048]{0:T(1024)S(1)} %iota_add_fusion, s32[2048]{0:T(1024)S(1)} %fusion.65, s32[1024]{0:T(1024)S(1)} %iota_add_fusion.1, s32[1024]{0:T(1024)S(1)} %fusion.72, pred[2048]{0:T(1024)(128)(4,1)S(1)} %fusion.69), kind=kLoop, calls=%fused_computation.25 | loop fusion | flops 8388608 | bytes 2123776 | tf_op jit(solution)/shard_map/and | solution.py:158
  121.2 9.8 %all-gather.4 = f32[8,2,3]{2,1,0:T(2,128)} all-gather(f32[1,2,3]{2,1,0:T(2,128)S(1)} %bitcast.141), channel_id=2, replica_groups=mesh['seq'=8,'head'=4] {'seq'}, dimensions={0}, use_global_device_ids=true | all-gather | bytes 216 | tf_op jit(solution)/shard_map/all_gather | solution.py:26
  135.1 3.5 collective-permute-start.1
  138.6 2.8 reshape.369
  144.4 3.6 copy.227
  148.1 3.1 collective-permute-start
  154.6 3.3 stack.4
  157.9 5.3 %all-to-all-start.1 = ((bf16[4,704,1024]{2,1,0:T(8,128)(2,1)}), bf16[4,704,1024]{2,1,0:T(8,128)(2,1)}, u32[]{:S(2)}, u32[]{:S(2)}) async-start(bf16[4,704,1024]{2,1,0:T(8,128)(2,1)} %stack.4), calls=%async_computation.1 | async-start | bytes 11534336 | tf_op jit(solution)/shard_map/all_to_all | solution.py:127
  167.7 3.2 fusion.32
  171.0 4.9 fusion.3
  176.0 5.6 %fusion.4 = f32[2,1024]{1,0:T(2,128)S(1)} fusion(f32[2,1024,2048]{2,1,0:T(8,128)S(1)} %get-tuple-element.215, f32[2,1024]{1,0:T(2,128)S(1)} %max.9, pred[1024,2048]{1,0:T(8,128)(4,1)S(1)} %copy-done.7), kind=kLoop, calls=%fused_computation.24 | loop fusion | flops 20969472 | bytes 18890752 | tf_op jit(solution)/shard_map/reduce_sum | solution.py:174
  183.6 4.3 fusion.29
  192.3 11.2 %fusion.43 = bf16[1024,2,128]{0,2,1:T(8,128)(2,1)} fusion(f32[1024,2,128]{0,2,1:T(8,128)} %copy.243, f32[1024,2,128]{0,2,1:T(8,128)} %convolution_bitcast_fusion, f32[2,1024,2048]{2,1,0:T(8,128)} %copy-done.3, f32[2,1024]{1,0:T(2,128)S(1)} %add.232, f32[2,1024]{1,0:T(2,128)S(1)} %max.9, pred[1024,2048]{1,0:T(8,128)(4,1)} %and_and_fusion, ...), kind=kOutput, calls=%fused_computation.64 | convolution fusion | flops 1101791232 | bytes 22560768 | tf_op jit(solution)/shard_map/hqk,khd->qhd/dot_general | solution.py:177
  207.6 116.1 %all-to-all-done.1 = bf16[4,704,1024]{2,1,0:T(8,128)(2,1)} async-done(((bf16[4,704,1024]{2,1,0:T(8,128)(2,1)}), bf16[4,704,1024]{2,1,0:T(8,128)(2,1)}, u32[]{:S(2)}, u32[]{:S(2)}) %all-to-all-start.1) | async-done | bytes 5767200 | tf_op jit(solution)/shard_map/all_to_all | solution.py:127
  323.8 4.1 all-to-all-start
  329.9 12.1 %all-to-all-done = bf16[4,256,256]{1,2,0:T(8,128)(2,1)} async-done(((bf16[4,256,256]{1,2,0:T(8,128)(2,1)}), bf16[4,256,256]{1,2,0:T(8,128)(2,1)}, u32[]{:S(2)}, u32[]{:S(2)}) %all-to-all-start) | async-done | bytes 524320 | tf_op jit(solution)/shard_map/all_to_all | solution.py:270
  346.7 44.7 %all-gather.17.cloned.1.call-done = bf16[1024,1024]{1,0:T(8,128)(2,1)} async-done(((bf16[256,1024]{1,0:T(8,128)(2,1)}), bf16[1024,1024]{1,0:T(8,128)(2,1)}) %all-gather.17.cloned.1.call-update) | async-done | bytes 2097168 | tf_op jit(solution)/shard_map/all_gather | solution.py:78
  391.4 5.0 fusion.85
  401.4 38.3 %all_to_all.15 = bf16[4,256,704]{1,2,0:T(8,128)(2,1)S(1)} all-to-all(bf16[4,256,704]{1,2,0:T(8,128)(2,1)} %copy.246), channel_id=1, replica_groups=mesh['seq'=8,'head'=4] {'head'}, dimensions={0} | all-to-all | bytes 2883584 | tf_op jit(solution)/shard_map/all_to_all | solution.py:278
  439.7 4.4 multiply_reduce_fusion
  445.5 3.0 slice.102
  451.1 8.8 %all-gather.5 = f32[8,4,2]{1,2,0:T(2,128)S(1)} all-gather(f32[1,4,2]{1,2,0:T(2,128)S(1)} %bitcast.145), channel_id=5, replica_groups=mesh['seq'=8,'head'=4] {'seq'}, dimensions={0}, use_global_device_ids=true | all-gather | bytes 288 | tf_op jit(solution)/shard_map/all_gather | solution.py:288
  460.5 29.7 %all-gather.19.cloned.1.call-done = bf16[1024,1024]{1,0:T(8,128)(2,1)} async-done(((bf16[256,1024]{1,0:T(8,128)(2,1)}), bf16[1024,1024]{1,0:T(8,128)(2,1)}) %all-gather.19.cloned.1.call-update) | async-done | bytes 2097168 | tf_op jit(solution)/shard_map/all_gather | solution.py:78
  490.3 12.9 %convolution_reduce_fusion = f32[1024]{0:T(1024)S(1)} fusion(bf16[1024,1024]{1,0:T(8,128)(2,1)} %all-gather.19.cloned.1.call-done, bf16[1024,4096]{1,0:T(8,128)(2,1)} %param.22), kind=kOutput, calls=%fused_computation.32 | convolution fusion | flops 8594127872 | bytes 10489856 | tf_op jit(solution)/shard_map/dot_general | solution.py:284
  503.2 10.1 %pmax.7 = f32[1024]{0:T(1024)} all-reduce(f32[1024]{0:T(1024)S(1)} %convolution_reduce_fusion), channel_id=1, replica_groups=mesh['seq'=8,'head'=4] {'head'}, use_global_device_ids=true, to_apply=%region_18.19 | all-reduce | flops 1024 | bytes 8192 | tf_op jit(solution)/shard_map/pmax | solution.py:287
  (279 shorter events, 85.5 us)
Async XLA Ops:
  7.2 384.3 %copy-start = (bf16[1024,2,704]{0,2,1:T(8,128)(2,1)S(1)}, bf16[1024,2,704]{0,2,1:T(8,128)(2,1)}, u32[]{:S(2)}) copy-start(bf16[1024,2,704]{0,2,1:T(8,128)(2,1)} %param.20) | copy-start | bytes 8650756
  7.2 3.5 copy-start.22
  7.2 4.6 copy-start.27
  7.2 4.8 copy-start.25
  7.2 4.9 copy-start.26
  7.2 5.6 %copy-start.19 = (f32[3,1024]{1,0:T(4,128)S(1)}, f32[3,1024]{1,0:T(4,128)}, u32[]{:S(2)}) copy-start(f32[3,1024]{1,0:T(4,128)} %param.24) | copy-start | bytes 36868
  7.2 51.1 %all-gather.13.cloned.1.call-start = ((), (), s32[]{:S(2)}) async-start(), calls=%async_computation.3 | async-start | bytes 2621440 | tf_op jit(solution)/shard_map/all_gather | solution.py:78
  8.0 175.0 %all-gather.21.cloned.1.call-start = ((), (), s32[]{:S(2)}) async-start(), calls=%async_computation.7 | async-start | bytes 1179648 | tf_op jit(solution)/shard_map/all_gather | solution.py:26
  12.2 51.7 %copy-start.30 = (s32[16]{0:T(128)}, s32[16]{0:T(128)S(1)}, u32[]{:S(2)}) copy-start(s32[16]{0:T(128)S(1)} %iota_add_fusion.2) | copy-start | bytes 196
  76.4 3.1 copy-start.6
  79.5 3.5 copy-start.29
  83.1 30.0 %copy-start.18 = (bf16[2,16,256]{2,1,0:T(8,128)(2,1)S(1)}, bf16[2,16,256]{2,1,0:T(8,128)(2,1)}, u32[]{:S(2)}) copy-start(bf16[2,16,256]{2,1,0:T(8,128)(2,1)} %param.23) | copy-start | bytes 49156
  113.0 70.0 %all-gather.23.cloned.1.call-start = ((), (), s32[]{:S(2)}) async-start(), calls=%async_computation.8 | async-start | bytes 1179648 | tf_op jit(solution)/shard_map/all_gather | solution.py:26
  121.2 20.2 %copy-start.20 = (f32[2,3]{1,0:T(2,128)}, f32[2,3]{1,0:T(2,128)S(1)}, u32[]{:S(2)}) copy-start(f32[2,3]{1,0:T(2,128)S(1)} %copy.239) | copy-start | bytes 76
  135.1 35.9 %collective-permute-start.1 = (bf16[1024,2,128]{2,0,1:T(8,128)(2,1)S(1)}, bf16[1024,2,128]{2,0,1:T(8,128)(2,1)}, u32[]{:S(2)}, u32[]{:S(2)}) collective-permute-start(bf16[1024,2,128]{2,0,1:T(8,128)(2,1)S(1)} %multiply_convert_fusion.4), channel_id=1, source_target_pairs={{0,4},{4,8},{8,12},{12,16},{16,20},{20,24},{24,28},{1,5},{5,9},{9,... | collective-permute-start | bytes 1572872 | tf_op jit(solution)/shard_map/ppermute | solution.py:21
  148.1 44.2 %collective-permute-start = (bf16[1024,2,128]{0,2,1:T(8,128)(2,1)}, bf16[1024,2,128]{0,2,1:T(8,128)(2,1)}, u32[]{:S(2)}, u32[]{:S(2)}) collective-permute-start(bf16[1024,2,128]{0,2,1:T(8,128)(2,1)} %bitcast.5), channel_id=1, source_target_pairs={{0,4},{4,8},{8,12},{12,16},{16,20},{20,24},{24,28},{1,5},{5,9},{9,... | collective-permute-start | bytes 1572872 | tf_op jit(solution)/shard_map/ppermute | solution.py:21
  157.9 8.0 %copy-start.15 = (bf16[16,2,128]{2,1,0:T(2,128)(2,1)S(1)}, bf16[16,2,128]{2,1,0:T(2,128)(2,1)}, u32[]{:S(2)}) copy-start(bf16[16,2,128]{2,1,0:T(2,128)(2,1)} %reshape_squeeze.6) | copy-start | bytes 24580
  157.9 165.9 %all-to-all-start.1 = ((bf16[4,704,1024]{2,1,0:T(8,128)(2,1)}), bf16[4,704,1024]{2,1,0:T(8,128)(2,1)}, u32[]{:S(2)}, u32[]{:S(2)}) async-start(bf16[4,704,1024]{2,1,0:T(8,128)(2,1)} %stack.4), calls=%async_computation.1 | async-start | bytes 11534336 | tf_op jit(solution)/shard_map/all_to_all | solution.py:127
  163.2 178.7 %all-gather.15.cloned.1.call-start = ((), (), s32[]{:S(2)}) async-start(), calls=%async_computation.4 | async-start | bytes 2621440 | tf_op jit(solution)/shard_map/all_gather | solution.py:123
  165.9 5.1 copy-start.7
  165.9 5.1 copy-start.12
  175.9 5.7 %copy-start.3 = (f32[2,1024,2048]{2,1,0:T(8,128)}, f32[2,1024,2048]{2,1,0:T(8,128)S(1)}, u32[]{:S(2)}) copy-start(f32[2,1024,2048]{2,1,0:T(8,128)S(1)} %get-tuple-element.215) | copy-start | bytes 50331652
  176.0 5.7 %copy-start.14 = (bf16[16,2,128]{2,1,0:T(2,128)(2,1)S(1)}, bf16[16,2,128]{2,1,0:T(2,128)(2,1)}, u32[]{:S(2)}) copy-start(bf16[16,2,128]{2,1,0:T(2,128)(2,1)} %reshape_squeeze.7) | copy-start | bytes 24580
  183.6 4.3 copy-start.9
  183.6 4.3 copy-start.11
  323.8 18.2 %all-to-all-start = ((bf16[4,256,256]{1,2,0:T(8,128)(2,1)}), bf16[4,256,256]{1,2,0:T(8,128)(2,1)}, u32[]{:S(2)}, u32[]{:S(2)}) async-start(bf16[4,256,256]{1,2,0:T(8,128)(2,1)} %copy.244), calls=%async_computation | async-start | bytes 1048576 | tf_op jit(solution)/shard_map/all_to_all | solution.py:270
  327.9 63.5 %all-gather.17.cloned.1.call-start = ((), (), s32[]{:S(2)}) async-start(), calls=%async_computation.5 | async-start | bytes 2621440 | tf_op jit(solution)/shard_map/all_gather | solution.py:78
  342.0 3.7 copy-start.17
  346.7 143.6 %all-gather.19.cloned.1.call-start = ((), (), s32[]{:S(2)}) async-start(), calls=%async_computation.6 | async-start | bytes 2621440 | tf_op jit(solution)/shard_map/all_gather | solution.py:78
  401.4 38.3 %copy-start.5 = (f32[256,1024]{1,0:T(8,128)S(1)}, f32[256,1024]{1,0:T(8,128)}, u32[]{:S(2)}) copy-start(f32[256,1024]{1,0:T(8,128)} %copy-done.4) | copy-start | bytes 3145732
  439.7 4.5 copy-start.16
  445.2 3.6 copy-start.2
  (10 other events, 12.9 us)
Sparse Core Ops, SparseCore 0:
  9.6 48.6 all-gather.12
  113.2 22.1 all-gather.20
  137.3 24.9 all-gather.22
  166.0 83.2 all-gather.14
  346.8 44.5 all-gather.16
  445.3 44.9 all-gather.18
